TPU v7x, 128 devices: a whole 4x4x4 slice. The times are simulated.
128 devices in a mesh: grp: 8 (over x_hi, z), vocab: 16 (over y, x_lo, core).
Axes of the slice: x: 4 (x_hi: 2, x_lo: 2; x = x_hi * 2 + x_lo), y: 4, z: 4, core: 2. Of those that a mesh axis runs over, the one named last changes fastest.
Arguments:
- hidden: bfloat16 [1024, 8192], P('grp', 'vocab')
- head_weight: bfloat16 [81920, 8192], P(('grp', 'vocab'))
- targets: int32 [1024], replicated, may hold values from 0 to 81919
- old_logprobs: float32 [1024], replicated
- loss_mask: int32 [1024], replicated, may hold values 0 or 1
- beam_lengths: int32 [128], replicated, may hold values from 1 to 24, 1024 in all
- beam_group: int32 [128], replicated, may hold values from 0 to 1, as said below
- rewards: float32 [128], replicated, may hold values from 0 to 1, as said below
Outputs:
- logprob: float32 [1024], replicated
- total_loss: float32 [], replicated
- head_grad: bfloat16 [81920, 8192], P(('grp', 'vocab'))
Inputs may be any that keep to these rules, and one draw needn't show every extreme that they name: `beam_group`: each of the 2 groups is named by exactly 64 beams. `rewards`: multiples of 1/8.
All inputs are finite; a program needn't handle non-finite values.
Results may differ from a plain program's by a relative error of at most 0.005.
Values may be sent and summed in bfloat16 or wider, within the bound.
No kernel may reach another device: no remote copies, remote signals or barrier semaphores. Data moves between devices by JAX's collectives and lax.ppermute only.
A program may use at most 128 MiB of HBM per device.

v0:
```python
import jax
import jax.numpy as jnp
from jax import lax
from jax.sharding import PartitionSpec as P

GROUP_BEAMS = 64


def policy_terms(logprob, old_logprobs, loss_mask, beam_lengths, beam_group, rewards):
    highest = lax.Precision.HIGHEST
    tok_count = logprob.shape[0]
    beam_count = beam_lengths.shape[0]
    group_count = beam_count // GROUP_BEAMS
    beam_ends = jnp.cumsum(beam_lengths)
    position = jnp.arange(tok_count, dtype=jnp.int32)
    beam_of = jnp.sum((position[:, None] >= beam_ends[None, :]).astype(jnp.int32), axis=1)
    token_beam = (beam_of[:, None] == jnp.arange(beam_count, dtype=jnp.int32)[None, :]).astype(
        jnp.float32
    )
    beam_onehot = (beam_group[:, None] == jnp.arange(group_count, dtype=jnp.int32)[None, :]).astype(
        jnp.float32
    )
    group_mean = jnp.dot(rewards, beam_onehot, precision=highest) / GROUP_BEAMS
    centred = rewards - jnp.dot(beam_onehot, group_mean, precision=highest)
    group_var = jnp.dot(centred * centred, beam_onehot, precision=highest) / GROUP_BEAMS
    advantage = centred / jnp.sqrt(jnp.dot(beam_onehot, group_var, precision=highest) + 1e-06)
    weight = loss_mask.astype(jnp.float32)
    counts = jnp.dot(weight, token_beam, precision=highest)
    token_adv = jnp.dot(token_beam, advantage, precision=highest)
    token_norm = jnp.dot(token_beam, jnp.maximum(counts, 1.0), precision=highest)
    ratios = jnp.exp(logprob - old_logprobs)
    clipped = jnp.clip(ratios, 0.8, 1.2)
    plain_term = ratios * token_adv
    bounded = clipped * token_adv
    token_share = weight / token_norm
    total_loss = -jnp.sum(token_share * jnp.minimum(plain_term, bounded))
    slopes = -token_share * jnp.where(plain_term <= bounded, plain_term, 0.0)
    return (total_loss, slopes)


def combine(mine, theirs):
    top = jnp.maximum(mine[0], theirs[0])
    total = mine[1] * jnp.exp(mine[0] - top) + theirs[1] * jnp.exp(theirs[0] - top)
    return jnp.stack([top, total, mine[2] + theirs[2]])


def butterfly(stats):
    for axis in ("vocab", "grp"):
        size = lax.axis_size(axis)
        step = 1
        while step < size:
            perm = [(i, i ^ step) for i in range(size)]
            stats = combine(stats, lax.ppermute(stats, axis, perm))
            step *= 2
    return (stats[0], stats[1], stats[2])


def shards(
    hidden, head_weight, targets, old_logprobs, loss_mask, beam_lengths, beam_group, rewards
):
    token_block = lax.all_gather(hidden, "grp", axis=0, tiled=True)
    features = lax.all_gather(token_block, "vocab", axis=1, tiled=True)
    shard = head_weight.shape[0]
    offset = (lax.axis_index("grp") * lax.axis_size("vocab") + lax.axis_index("vocab")) * shard
    vocab_ids = offset + jnp.arange(shard, dtype=jnp.int32)
    logits = lax.dot_general(
        features, head_weight, (((1,), (1,)), ((), ())), preferred_element_type=jnp.float32
    )
    hits = targets[:, None] == vocab_ids[None, :]
    picked = jnp.sum(jnp.where(hits, logits, 0.0), axis=1)
    local_top = jnp.max(logits, axis=1)
    local_sum = jnp.sum(jnp.exp(logits - local_top[:, None]), axis=1)
    top, total, target_logit = butterfly(jnp.stack([local_top, local_sum, picked]))
    log_total = top + jnp.log(total)
    logprob = target_logit - log_total
    total_loss, slopes = policy_terms(
        logprob, old_logprobs, loss_mask, beam_lengths, beam_group, rewards
    )
    grads = (
        slopes[:, None] * (hits.astype(jnp.float32) - jnp.exp(logits - log_total[:, None]))
    ).astype(jnp.bfloat16)
    head_grad = lax.dot_general(
        grads, features, (((0,), (0,)), ((), ())), preferred_element_type=jnp.float32
    )
    return (logprob, total_loss, head_grad.astype(jnp.bfloat16))


def solution(mesh):
    in_specs = (P("grp", "vocab"), P(("grp", "vocab"), None), P(), P(), P(), P(), P(), P())
    out_specs = (P(), P(), P(("grp", "vocab"), None))
    return jax.shard_map(shards, mesh=mesh, in_specs=in_specs, out_specs=out_specs, check_vma=False)
```

profile of v0, /device:TPU:0, one launch (start us, length us, event | category | flops | bytes accessed | tf_op | source)
XLA Modules:
  0.0 226.4 jit_solution(9675438265571959442)
XLA Ops:
  7.2 0.7 all-gather.3.cloned.1.call-update
  7.9 51.4 %all-gather.3.cloned.1.call-done = bf16[1024,512]{1,0:T(8,128)(2,1)} async-done(((bf16[128,512]{1,0:T(8,128)(2,1)}), bf16[1024,512]{1,0:T(8,128)(2,1)}) %all-gather.3.cloned.1.call-update) | async-done | bytes 1048592 | tf_op jit(solution)/shard_map/all_gather | solution.py:61
  59.3 0.7 convert_element_type.17
  60.0 0.8 copy.13
  60.8 0.2 reduce-window.8
  61.1 0.2 convert_reduce_fusion
  61.3 90.0 %all-gather.5.cloned.1.call-done = bf16[1024,8192]{1,0:T(8,128)(2,1)} async-done(((bf16[1024,512]{1,0:T(8,128)(2,1)}), bf16[1024,8192]{1,0:T(8,128)(2,1)}) %all-gather.5.cloned.1.call-update) | async-done | bytes 16777232 | tf_op jit(solution)/shard_map/all_gather | solution.py:62
  151.3 16.3 %fusion.53 = (f32[1024]{0:T(1024)S(1)}, f32[1024,640]{0,1:T(8,128)S(1)}) fusion(bf16[1024,8192]{1,0:T(8,128)(2,1)} %all-gather.5.cloned.1.call-done, bf16[640,8192]{1,0:T(8,128)(2,1)} %param.9), kind=kOutput, calls=%fused_computation.105 | convolution fusion | flops 10738072576 | bytes 29888512 | tf_op jit(solution)/shard_map/dot_general | solution.py:66
  167.6 0.6 exponential_reduce_fusion
  168.3 0.3 collective-permute-start
  168.6 0.4 fusion.19
  169.0 0.6 collective-permute-done
  169.6 1.4 collective-permute-start.1
  171.0 0.4 fusion.21
  171.4 2.0 collective-permute-done.1
  173.5 1.6 collective-permute-start.2
  175.1 0.2 fusion.15
  175.3 2.1 collective-permute-done.2
  177.4 2.8 %collective-permute-start.3 = (f32[3,1024]{1,0:T(4,128)S(1)}, f32[3,1024]{1,0:T(4,128)S(1)}, u32[]{:S(2)}, u32[]{:S(2)}) collective-permute-start(f32[3,1024]{1,0:T(4,128)S(1)} %pad_maximum_fusion.3), channel_id=1, source_target_pairs={{0,8},{1,9},{2,10},{3,11},{4,12},{5,13},{6,14},{7,15},{8,0},{9,1},... | collective-permute-start | bytes 36872 | tf_op jit(solution)/shard_map/ppermute | solution.py:53
  180.2 0.2 fusion.13
  180.4 2.3 %collective-permute-done.3 = f32[3,1024]{1,0:T(4,128)S(1)} collective-permute-done((f32[3,1024]{1,0:T(4,128)S(1)}, f32[3,1024]{1,0:T(4,128)S(1)}, u32[]{:S(2)}, u32[]{:S(2)}) %collective-permute-start.3) | collective-permute-done | bytes 12320 | tf_op jit(solution)/shard_map/ppermute | solution.py:53
  182.8 1.6 collective-permute-start.4
  184.4 0.2 fusion.12
  184.6 2.0 collective-permute-done.4
  186.6 3.2 %collective-permute-start.5 = (f32[3,1024]{1,0:T(4,128)S(1)}, f32[3,1024]{1,0:T(4,128)S(1)}, u32[]{:S(2)}, u32[]{:S(2)}) collective-permute-start(f32[3,1024]{1,0:T(4,128)S(1)} %pad_maximum_fusion.5), channel_id=1, source_target_pairs={{0,32},{16,48},{32,0},{48,16},{64,96},{80,112},{96,64},{112,80},{1... | collective-permute-start | bytes 36872 | tf_op jit(solution)/shard_map/ppermute | solution.py:53
  189.9 0.2 fusion.17
  190.1 1.9 collective-permute-done.5
  192.0 3.2 %collective-permute-start.6 = (f32[3,1024]{1,0:T(4,128)S(1)}, f32[3,1024]{1,0:T(4,128)S(1)}, u32[]{:S(2)}, u32[]{:S(2)}) collective-permute-start(f32[3,1024]{1,0:T(4,128)S(1)} %pad_maximum_fusion.6), channel_id=1, source_target_pairs={{0,64},{16,80},{32,96},{48,112},{64,0},{80,16},{96,32},{112,48},{1... | collective-permute-start | bytes 36872 | tf_op jit(solution)/shard_map/ppermute | solution.py:53
  195.2 0.4 fusion.20
  195.7 1.8 collective-permute-done.6
  197.6 0.6 multiply_reduce_fusion
  198.9 19.5 %convolution_convert_fusion = bf16[640,8192]{1,0:T(8,128)(2,1)} fusion(bf16[1024,8192]{1,0:T(8,128)(2,1)} %all-gather.5.cloned.1.call-done, f32[1024,640]{0,1:T(8,128)S(1)} %get-tuple-element.58, f32[1024]{0:T(1024)S(1)} %get-tuple-element.7, f32[1024]{0:T(1024)S(1)} %get-tuple-element.5, s32[1024]{0:T(1024)S(1)} %copy-done.3, s32[640]{0:T(1024)S(1)} %iota_add_fusion), kind=kOutput, calls=%fused_computation | convolution fusion | flops 10746593280 | bytes 29899264 | tf_op jit(solution)/shard_map/dot_general | solution.py:82
  (32 shorter events, 0.6 us)
Async XLA Ops:
  7.2 52.1 %all-gather.3.cloned.1.call-start = ((), (), s32[]{:S(2)}) async-start(), calls=%async_computation | async-start | bytes 1179648 | tf_op jit(solution)/shard_map/all_gather | solution.py:61
  7.9 143.4 %all-gather.5.cloned.1.call-start = ((), (), s32[]{:S(2)}) async-start(), calls=%async_computation.1 | async-start | bytes 17825792 | tf_op jit(solution)/shard_map/all_gather | solution.py:62
  61.3 106.3 %copy-start.3 = (s32[1024]{0:T(1024)S(1)}, s32[1024]{0:T(1024)}, u32[]{:S(2)}) copy-start(s32[1024]{0:T(1024)} %param.10) | copy-start | bytes 12292
  167.6 7.5 %copy-start.4 = (f32[128]{0:T(128)S(1)}, f32[128]{0:T(128)}, u32[]{:S(2)}) copy-start(f32[128]{0:T(128)} %param.15) | copy-start | bytes 1540
  167.6 7.5 %copy-start.5 = (s32[128]{0:T(128)S(1)}, s32[128]{0:T(128)}, u32[]{:S(2)}) copy-start(s32[128]{0:T(128)} %param.14) | copy-start | bytes 1540
  167.6 29.9 %copy-start = (s32[1024]{0:T(1024)S(1)}, s32[1024]{0:T(1024)}, u32[]{:S(2)}) copy-start(s32[1024]{0:T(1024)} %param.12) | copy-start | bytes 12292
  167.6 29.9 %copy-start.1 = (f32[1024]{0:T(1024)S(1)}, f32[1024]{0:T(1024)}, u32[]{:S(2)}) copy-start(f32[1024]{0:T(1024)} %param.11) | copy-start | bytes 12292
  168.3 1.3 collective-permute-start
  169.6 3.8 %collective-permute-start.1 = (f32[3,1024]{1,0:T(4,128)S(1)}, f32[3,1024]{1,0:T(4,128)S(1)}, u32[]{:S(2)}, u32[]{:S(2)}) collective-permute-start(f32[3,1024]{1,0:T(4,128)S(1)} %pad_maximum_fusion.1), channel_id=1, source_target_pairs={{0,2},{1,3},{2,0},{3,1},{4,6},{5,7},{6,4},{7,5},{8,10},{9,11},{10,... | collective-permute-start | bytes 36872 | tf_op jit(solution)/shard_map/ppermute | solution.py:53
  173.5 3.8 %collective-permute-start.2 = (f32[3,1024]{1,0:T(4,128)S(1)}, f32[3,1024]{1,0:T(4,128)S(1)}, u32[]{:S(2)}, u32[]{:S(2)}) collective-permute-start(f32[3,1024]{1,0:T(4,128)S(1)} %pad_maximum_fusion.2), channel_id=1, source_target_pairs={{0,4},{1,5},{2,6},{3,7},{4,0},{5,1},{6,2},{7,3},{8,12},{9,13},{10,... | collective-permute-start | bytes 36872 | tf_op jit(solution)/shard_map/ppermute | solution.py:53
  177.4 5.3 %collective-permute-start.3 = (f32[3,1024]{1,0:T(4,128)S(1)}, f32[3,1024]{1,0:T(4,128)S(1)}, u32[]{:S(2)}, u32[]{:S(2)}) collective-permute-start(f32[3,1024]{1,0:T(4,128)S(1)} %pad_maximum_fusion.3), channel_id=1, source_target_pairs={{0,8},{1,9},{2,10},{3,11},{4,12},{5,13},{6,14},{7,15},{8,0},{9,1},... | collective-permute-start | bytes 36872 | tf_op jit(solution)/shard_map/ppermute | solution.py:53
  182.8 3.8 %collective-permute-start.4 = (f32[3,1024]{1,0:T(4,128)S(1)}, f32[3,1024]{1,0:T(4,128)S(1)}, u32[]{:S(2)}, u32[]{:S(2)}) collective-permute-start(f32[3,1024]{1,0:T(4,128)S(1)} %pad_maximum_fusion.4), channel_id=1, source_target_pairs={{0,16},{16,0},{32,48},{48,32},{64,80},{80,64},{96,112},{112,96},{1... | collective-permute-start | bytes 36872 | tf_op jit(solution)/shard_map/ppermute | solution.py:53
  186.6 5.3 %collective-permute-start.5 = (f32[3,1024]{1,0:T(4,128)S(1)}, f32[3,1024]{1,0:T(4,128)S(1)}, u32[]{:S(2)}, u32[]{:S(2)}) collective-permute-start(f32[3,1024]{1,0:T(4,128)S(1)} %pad_maximum_fusion.5), channel_id=1, source_target_pairs={{0,32},{16,48},{32,0},{48,16},{64,96},{80,112},{96,64},{112,80},{1... | collective-permute-start | bytes 36872 | tf_op jit(solution)/shard_map/ppermute | solution.py:53
  192.0 5.5 %collective-permute-start.6 = (f32[3,1024]{1,0:T(4,128)S(1)}, f32[3,1024]{1,0:T(4,128)S(1)}, u32[]{:S(2)}, u32[]{:S(2)}) collective-permute-start(f32[3,1024]{1,0:T(4,128)S(1)} %pad_maximum_fusion.6), channel_id=1, source_target_pairs={{0,64},{16,80},{32,96},{48,112},{64,0},{80,16},{96,32},{112,48},{1... | collective-permute-start | bytes 36872 | tf_op jit(solution)/shard_map/ppermute | solution.py:53
  197.6 20.8 %copy-start.2 = (f32[1024]{0:T(1024)}, f32[1024]{0:T(1024)S(1)}, u32[]{:S(2)}) copy-start(f32[1024]{0:T(1024)S(1)} %get-tuple-element.6) | copy-start | bytes 12292
Sparse Core Ops, SparseCore 0:
  10.3 48.9 all-gather.2
  61.0 90.2 all-gather.4
where the time goes:
time: 227 us; the launch traced here: 226 us
  waiting for transfers between devices  155 us (68%)
  matrix products  37.8 us (17%)
  between operations  16 us (7%)
  starting transfers between devices  14.3 us (6%)
  other arithmetic  2.78 us (1%)
    all_gather x1, waiting for transfers between devices, shards(): features = lax.all_gather(token_block, 'vocab', axis=1, tiled=True)  90 us
    all_gather x1, waiting for transfers between devices, shards(): token_block = lax.all_gather(hidden, 'grp', axis=0, tiled=True)  51.4 us
    dot_general x1, matrix products, shards(): lax.dot_general(grads, features, (((0,), (0,)), ((), ())), preferred_elem...  19.5 us
    dot_general x1, matrix products, shards(): lax.dot_general(features, head_weight, (((1,), (1,)), ((), ())), preferre...  16.3 us
    ppermute x7, starting transfers between devices, butterfly(): stats = combine(stats, lax.ppermute(stats, axis, perm))  14.2 us
    ppermute x7, waiting for transfers between devices, butterfly(): stats = combine(stats, lax.ppermute(stats, axis, perm))  12.7 us
  transfers between devices with their start and end apart: 9, of which 9 were waited for; matrix products, arithmetic and copies ran while one was open for 2% of the time, Pallas kernels for 0%

commit v1 on v0

--- a/solution.py
+++ b/solution.py
@@ -58,7 +58,12 @@
 def shards(
     hidden, head_weight, targets, old_logprobs, loss_mask, beam_lengths, beam_group, rewards
 ):
-    token_block = lax.all_gather(hidden, "grp", axis=0, tiled=True)
+    token_block = jnp.concatenate(
+        jax.lax.all_to_all(
+            jnp.stack([hidden for _ in range(jax.lax.axis_size("grp"))]), "grp", 0, 0
+        ),
+        axis=0,
+    )
     features = lax.all_gather(token_block, "vocab", axis=1, tiled=True)
     shard = head_weight.shape[0]
     offset = (lax.axis_index("grp") * lax.axis_size("vocab") + lax.axis_index("vocab")) * shard

time: 227 us -> 198 us (0.87)
  waiting for transfers between devices: 155 us -> 101 us
  blocking collectives: 0 us -> 24.9 us
    all_gather x1 -> x0, waiting for transfers between devices: 51.4 us -> none  [shards(): token_block = lax.all_gather(hidden, 'grp', axis=0, tiled=True)]
    all_to_all x0 -> x1, blocking collectives: none -> 24.9 us  [shards(): jax.lax.all_to_all(jnp.stack([hidden for _ in range(jax.lax.axis_size('gr...]
  transfers between devices with their start and end apart: 9 -> 8, of which waited for: 9 -> 8; matrix products, arithmetic and copies ran while one was open for 2% -> 1% of each run, Pallas kernels for 0% -> 0%
where the time goes in v1:
time: 198 us; the launch traced here: 197 us
  waiting for transfers between devices  101 us (51%)
  matrix products  37.8 us (19%)
  blocking collectives  24.9 us (13%)
  between operations  16 us (8%)
  starting transfers between devices  14.2 us (7%)
  other arithmetic  2.09 us (1%)
    all_gather x1, waiting for transfers between devices, shards(): features = lax.all_gather(token_block, 'vocab', axis=1, tiled=True)  88.4 us
    all_to_all x1, blocking collectives, shards(): jax.lax.all_to_all(jnp.stack([hidden for _ in range(jax.lax.axis_size('gr...  24.9 us
    dot_general x1, matrix products, shards(): lax.dot_general(grads, features, (((0,), (0,)), ((), ())), preferred_elem...  19.5 us
    dot_general x1, matrix products, shards(): lax.dot_general(features, head_weight, (((1,), (1,)), ((), ())), preferre...  16.3 us
    ppermute x7, starting transfers between devices, butterfly(): stats = combine(stats, lax.ppermute(stats, axis, perm))  14.2 us
    ppermute x7, waiting for transfers between devices, butterfly(): stats = combine(stats, lax.ppermute(stats, axis, perm))  12.7 us
  transfers between devices with their start and end apart: 8, of which 8 were waited for; matrix products, arithmetic and copies ran while one was open for 1% of the time, Pallas kernels for 0%

profile of v1, /device:TPU:0, one launch (start us, length us, event | category | flops | bytes accessed | tf_op | source)
XLA Modules:
  0.0 197.3 jit_solution(12240403941656959560)
XLA Ops:
  7.2 1.0 stack.22
  8.2 24.9 %all_to_all.5 = bf16[8,128,512]{2,1,0:T(8,128)(2,1)} all-to-all(bf16[8,128,512]{2,1,0:T(8,128)(2,1)S(1)} %stack.22), channel_id=1, replica_groups=mesh['grp'=8,'vocab'=16] {'grp'}, dimensions={0} | all-to-all | bytes 2097152 | tf_op jit(solution)/shard_map/all_to_all | solution.py:62
  33.2 0.1 copy.13
  33.3 0.2 reduce-window.8
  33.5 0.1 reduce
  33.6 0.2 convert_reduce_fusion
  33.9 88.4 %all-gather.2.cloned.1.call-done = bf16[1024,8192]{1,0:T(8,128)(2,1)} async-done(((bf16[1024,512]{1,0:T(8,128)(2,1)}), bf16[1024,8192]{1,0:T(8,128)(2,1)}) %all-gather.2.cloned.1.call-update) | async-done | bytes 16777232 | tf_op jit(solution)/shard_map/all_gather | solution.py:67
  122.3 16.3 %fusion.53 = (f32[1024]{0:T(1024)S(1)}, f32[1024,640]{0,1:T(8,128)S(1)}) fusion(bf16[1024,8192]{1,0:T(8,128)(2,1)} %all-gather.2.cloned.1.call-done, bf16[640,8192]{1,0:T(8,128)(2,1)} %param.9), kind=kOutput, calls=%fused_computation.105 | convolution fusion | flops 10738072576 | bytes 29888512 | tf_op jit(solution)/shard_map/dot_general | solution.py:71
  138.6 0.6 exponential_reduce_fusion
  139.3 0.3 collective-permute-start
  139.6 0.4 fusion.19
  140.0 0.6 collective-permute-done
  140.6 1.4 collective-permute-start.1
  142.0 0.4 fusion.21
  142.4 2.0 %collective-permute-done.1 = f32[3,1024]{1,0:T(4,128)S(1)} collective-permute-done((f32[3,1024]{1,0:T(4,128)S(1)}, f32[3,1024]{1,0:T(4,128)S(1)}, u32[]{:S(2)}, u32[]{:S(2)}) %collective-permute-start.1) | collective-permute-done | bytes 12320 | tf_op jit(solution)/shard_map/ppermute | solution.py:53
  144.5 1.6 collective-permute-start.2
  146.0 0.2 fusion.15
  146.2 2.1 %collective-permute-done.2 = f32[3,1024]{1,0:T(4,128)S(1)} collective-permute-done((f32[3,1024]{1,0:T(4,128)S(1)}, f32[3,1024]{1,0:T(4,128)S(1)}, u32[]{:S(2)}, u32[]{:S(2)}) %collective-permute-start.2) | collective-permute-done | bytes 12320 | tf_op jit(solution)/shard_map/ppermute | solution.py:53
  148.3 2.8 %collective-permute-start.3 = (f32[3,1024]{1,0:T(4,128)S(1)}, f32[3,1024]{1,0:T(4,128)S(1)}, u32[]{:S(2)}, u32[]{:S(2)}) collective-permute-start(f32[3,1024]{1,0:T(4,128)S(1)} %pad_maximum_fusion.3), channel_id=1, source_target_pairs={{0,8},{1,9},{2,10},{3,11},{4,12},{5,13},{6,14},{7,15},{8,0},{9,1},... | collective-permute-start | bytes 36872 | tf_op jit(solution)/shard_map/ppermute | solution.py:53
  151.1 0.2 fusion.13
  151.3 2.3 %collective-permute-done.3 = f32[3,1024]{1,0:T(4,128)S(1)} collective-permute-done((f32[3,1024]{1,0:T(4,128)S(1)}, f32[3,1024]{1,0:T(4,128)S(1)}, u32[]{:S(2)}, u32[]{:S(2)}) %collective-permute-start.3) | collective-permute-done | bytes 12320 | tf_op jit(solution)/shard_map/ppermute | solution.py:53
  153.7 1.6 collective-permute-start.4
  155.4 0.2 fusion.12
  155.5 2.0 %collective-permute-done.4 = f32[3,1024]{1,0:T(4,128)S(1)} collective-permute-done((f32[3,1024]{1,0:T(4,128)S(1)}, f32[3,1024]{1,0:T(4,128)S(1)}, u32[]{:S(2)}, u32[]{:S(2)}) %collective-permute-start.4) | collective-permute-done | bytes 12320 | tf_op jit(solution)/shard_map/ppermute | solution.py:53
  157.6 3.2 %collective-permute-start.5 = (f32[3,1024]{1,0:T(4,128)S(1)}, f32[3,1024]{1,0:T(4,128)S(1)}, u32[]{:S(2)}, u32[]{:S(2)}) collective-permute-start(f32[3,1024]{1,0:T(4,128)S(1)} %pad_maximum_fusion.5), channel_id=1, source_target_pairs={{0,32},{16,48},{32,0},{48,16},{64,96},{80,112},{96,64},{112,80},{1... | collective-permute-start | bytes 36872 | tf_op jit(solution)/shard_map/ppermute | solution.py:53
  160.8 0.2 fusion.17
  161.0 1.9 collective-permute-done.5
  163.0 3.2 %collective-permute-start.6 = (f32[3,1024]{1,0:T(4,128)S(1)}, f32[3,1024]{1,0:T(4,128)S(1)}, u32[]{:S(2)}, u32[]{:S(2)}) collective-permute-start(f32[3,1024]{1,0:T(4,128)S(1)} %pad_maximum_fusion.6), channel_id=1, source_target_pairs={{0,64},{16,80},{32,96},{48,112},{64,0},{80,16},{96,32},{112,48},{1... | collective-permute-start | bytes 36872 | tf_op jit(solution)/shard_map/ppermute | solution.py:53
  166.2 0.4 fusion.20
  166.7 1.8 collective-permute-done.6
  168.6 0.6 multiply_reduce_fusion
  169.8 19.5 %convolution_convert_fusion = bf16[640,8192]{1,0:T(8,128)(2,1)} fusion(bf16[1024,8192]{1,0:T(8,128)(2,1)} %all-gather.2.cloned.1.call-done, f32[1024,640]{0,1:T(8,128)S(1)} %get-tuple-element.58, f32[1024]{0:T(1024)S(1)} %get-tuple-element.7, f32[1024]{0:T(1024)S(1)} %get-tuple-element.5, s32[1024]{0:T(1024)S(1)} %copy-done.3, s32[640]{0:T(1024)S(1)} %iota_add_fusion), kind=kOutput, calls=%fused_computation | convolution fusion | flops 10746593280 | bytes 29899264 | tf_op jit(solution)/shard_map/dot_general | solution.py:87
  (33 shorter events, 0.5 us)
Async XLA Ops:
  7.2 26.0 %copy-start = (s32[1024]{0:T(1024)S(1)}, s32[1024]{0:T(1024)}, u32[]{:S(2)}) copy-start(s32[1024]{0:T(1024)} %param.12) | copy-start | bytes 12292
  7.2 26.0 %copy-start.4 = (s32[128]{0:T(128)S(1)}, s32[128]{0:T(128)}, u32[]{:S(2)}) copy-start(s32[128]{0:T(128)} %param.13) | copy-start | bytes 1540
  7.2 115.1 %all-gather.2.cloned.1.call-start = ((), (), s32[]{:S(2)}) async-start(), calls=%async_computation.1 | async-start | bytes 17825792 | tf_op jit(solution)/shard_map/all_gather | solution.py:67
  33.8 104.8 %copy-start.3 = (s32[1024]{0:T(1024)S(1)}, s32[1024]{0:T(1024)}, u32[]{:S(2)}) copy-start(s32[1024]{0:T(1024)} %param.10) | copy-start | bytes 12292
  138.6 7.5 %copy-start.5 = (f32[128]{0:T(128)S(1)}, f32[128]{0:T(128)}, u32[]{:S(2)}) copy-start(f32[128]{0:T(128)} %param.15) | copy-start | bytes 1540
  138.6 7.5 %copy-start.6 = (s32[128]{0:T(128)S(1)}, s32[128]{0:T(128)}, u32[]{:S(2)}) copy-start(s32[128]{0:T(128)} %param.14) | copy-start | bytes 1540
  138.6 29.9 %copy-start.1 = (f32[1024]{0:T(1024)S(1)}, f32[1024]{0:T(1024)}, u32[]{:S(2)}) copy-start(f32[1024]{0:T(1024)} %param.11) | copy-start | bytes 12292
  139.3 1.3 collective-permute-start
  140.6 3.8 %collective-permute-start.1 = (f32[3,1024]{1,0:T(4,128)S(1)}, f32[3,1024]{1,0:T(4,128)S(1)}, u32[]{:S(2)}, u32[]{:S(2)}) collective-permute-start(f32[3,1024]{1,0:T(4,128)S(1)} %pad_maximum_fusion.1), channel_id=1, source_target_pairs={{0,2},{1,3},{2,0},{3,1},{4,6},{5,7},{6,4},{7,5},{8,10},{9,11},{10,... | collective-permute-start | bytes 36872 | tf_op jit(solution)/shard_map/ppermute | solution.py:53
  144.5 3.8 %collective-permute-start.2 = (f32[3,1024]{1,0:T(4,128)S(1)}, f32[3,1024]{1,0:T(4,128)S(1)}, u32[]{:S(2)}, u32[]{:S(2)}) collective-permute-start(f32[3,1024]{1,0:T(4,128)S(1)} %pad_maximum_fusion.2), channel_id=1, source_target_pairs={{0,4},{1,5},{2,6},{3,7},{4,0},{5,1},{6,2},{7,3},{8,12},{9,13},{10,... | collective-permute-start | bytes 36872 | tf_op jit(solution)/shard_map/ppermute | solution.py:53
  148.3 5.3 %collective-permute-start.3 = (f32[3,1024]{1,0:T(4,128)S(1)}, f32[3,1024]{1,0:T(4,128)S(1)}, u32[]{:S(2)}, u32[]{:S(2)}) collective-permute-start(f32[3,1024]{1,0:T(4,128)S(1)} %pad_maximum_fusion.3), channel_id=1, source_target_pairs={{0,8},{1,9},{2,10},{3,11},{4,12},{5,13},{6,14},{7,15},{8,0},{9,1},... | collective-permute-start | bytes 36872 | tf_op jit(solution)/shard_map/ppermute | solution.py:53
  153.7 3.8 %collective-permute-start.4 = (f32[3,1024]{1,0:T(4,128)S(1)}, f32[3,1024]{1,0:T(4,128)S(1)}, u32[]{:S(2)}, u32[]{:S(2)}) collective-permute-start(f32[3,1024]{1,0:T(4,128)S(1)} %pad_maximum_fusion.4), channel_id=1, source_target_pairs={{0,16},{16,0},{32,48},{48,32},{64,80},{80,64},{96,112},{112,96},{1... | collective-permute-start | bytes 36872 | tf_op jit(solution)/shard_map/ppermute | solution.py:53
  157.6 5.3 %collective-permute-start.5 = (f32[3,1024]{1,0:T(4,128)S(1)}, f32[3,1024]{1,0:T(4,128)S(1)}, u32[]{:S(2)}, u32[]{:S(2)}) collective-permute-start(f32[3,1024]{1,0:T(4,128)S(1)} %pad_maximum_fusion.5), channel_id=1, source_target_pairs={{0,32},{16,48},{32,0},{48,16},{64,96},{80,112},{96,64},{112,80},{1... | collective-permute-start | bytes 36872 | tf_op jit(solution)/shard_map/ppermute | solution.py:53
  163.0 5.5 %collective-permute-start.6 = (f32[3,1024]{1,0:T(4,128)S(1)}, f32[3,1024]{1,0:T(4,128)S(1)}, u32[]{:S(2)}, u32[]{:S(2)}) collective-permute-start(f32[3,1024]{1,0:T(4,128)S(1)} %pad_maximum_fusion.6), channel_id=1, source_target_pairs={{0,64},{16,80},{32,96},{48,112},{64,0},{80,16},{96,32},{112,48},{1... | collective-permute-start | bytes 36872 | tf_op jit(solution)/shard_map/ppermute | solution.py:53
  168.6 20.8 %copy-start.2 = (f32[1024]{0:T(1024)}, f32[1024]{0:T(1024)S(1)}, u32[]{:S(2)}) copy-start(f32[1024]{0:T(1024)S(1)} %get-tuple-element.6) | copy-start | bytes 12292
Sparse Core Ops, SparseCore 0:
  33.3 88.9 all-gather.1
